TPU v7x, 512 devices: a whole 4x4x16 slice. The times are simulated.
512 devices in a mesh: dp: 32 (over y, z_hi, core), mp: 16 (over z_lo, x).
Axes of the slice: x: 4, y: 4, z: 16 (z_hi: 4, z_lo: 4; z = z_hi * 4 + z_lo), core: 2. Of those that a mesh axis runs over, the one named last changes fastest.
Arguments:
- inputs: bfloat16 [16384, 4096], P('mp', 'dp'), may hold values from -6 to 6
- cotangent: bfloat16 [16384, 4096], P('mp', 'dp'), may hold values from -6 to 6
- r_factor: bfloat16 [1, 128, 128, 128], P(None, 'mp'), may hold values from -0.5 to 0.5
- l_factor: bfloat16 [1, 128, 128, 128], P(None, 'mp'), may hold values from -0.5 to 0.5
Outputs:
- outputs: bfloat16 [16384, 4096], P('mp', 'dp')
- grad_inputs: bfloat16 [16384, 4096], P('mp', 'dp')
- grad_r: float32 [1, 128, 128, 128], P(None, 'mp', 'dp')
- grad_l: float32 [1, 128, 128, 128], P(None, 'mp', 'dp')
All inputs are finite; a program needn't handle non-finite values.
Results may differ from a plain program's by a relative error of at most 0.0063.
Values may be sent and summed in bfloat16 or wider, within the bound.
No kernel may reach another device: no remote copies, remote signals or barrier semaphores. Data moves between devices by JAX's collectives and lax.ppermute only.
A program may use at most 64 MiB of HBM per device.

v0:
```python
import jax
import jax.numpy as jnp
from jax import lax
from jax.sharding import PartitionSpec as P

LAYERS = 1


def activate(values):
    return jax.nn.gelu(values, approximate=True)


def second_product(received, left):
    return jnp.einsum("ijt,jim->jmt", received, left, preferred_element_type=jnp.float32)


def left_apply(left, received):
    return (received, second_product(received, left))


def first_product(current, right):
    return jnp.einsum("ikt,ikj->ijt", current, right, preferred_element_type=jnp.float32).astype(
        jnp.bfloat16
    )


def forward_layer(current, right, left):
    first_out = first_product(current, right)
    return left_apply(
        left, lax.all_to_all(first_out, "mp", split_axis=1, concat_axis=0, tiled=True)
    )


def shards(inputs, cotangent, r_factor, l_factor):
    block_count = r_factor.shape[1]
    block_size = r_factor.shape[2]
    tokens_here = inputs.shape[1]
    scale = float(lax.axis_size("dp") * tokens_here) ** (-0.5)
    current = inputs.reshape(block_count, block_size, tokens_here)
    layer_index = 0
    received, pre_act = forward_layer(current, r_factor[layer_index], l_factor[layer_index])
    saved = [(current, received, pre_act)]
    current = activate(pre_act).astype(jnp.bfloat16)
    outputs = current.reshape(block_count * block_size, tokens_here)
    grad_now = cotangent.reshape(block_count, block_size, tokens_here)
    parts_r = [None] * LAYERS
    parts_l = [None] * LAYERS
    for layer_index in reversed(range(LAYERS)):
        right = r_factor[layer_index]
        left = l_factor[layer_index]
        layer_in = saved[layer_index][0]
        received = saved[layer_index][1]
        pre_act = saved[layer_index][2]
        back_fn = jax.vjp(activate, pre_act)[1]
        grad_pre = back_fn(grad_now.astype(jnp.float32))[0].astype(jnp.bfloat16)
        term_l = (
            jnp.einsum("ijt,jmt->jim", received, grad_pre, preferred_element_type=jnp.float32)
            * scale
        )
        parts_l[layer_index] = lax.psum_scatter(term_l, "dp", scatter_dimension=1, tiled=True)
        grad_first = jnp.einsum(
            "jmt,jim->ijt", grad_pre, left, preferred_element_type=jnp.float32
        ).astype(jnp.bfloat16)

        def apply_back(returned, right=right):
            spread = jnp.einsum("ijt,ikj->ikt", returned, right, preferred_element_type=jnp.float32)
            return (returned, spread.astype(jnp.bfloat16))

        returned, grad_now = apply_back(
            lax.all_to_all(grad_first, "mp", split_axis=0, concat_axis=1, tiled=True)
        )
        term_r = (
            jnp.einsum("ikt,ijt->ikj", layer_in, returned, preferred_element_type=jnp.float32)
            * scale
        )
        parts_r[layer_index] = lax.psum_scatter(term_r, "dp", scatter_dimension=1, tiled=True)
    stack_r = jnp.stack(parts_r, 0)
    stack_l = jnp.stack(parts_l, 0)
    grad_inputs = grad_now.reshape(block_count * block_size, tokens_here)
    return (outputs, grad_inputs, stack_r, stack_l)


def solution(mesh):
    placed = (P("mp", "dp"), P("mp", "dp"), P(None, "mp", None, None), P(None, "mp", None, None))
    return jax.shard_map(
        shards,
        mesh=mesh,
        in_specs=placed,
        out_specs=(
            P("mp", "dp"),
            P("mp", "dp"),
            P(None, "mp", "dp", None),
            P(None, "mp", "dp", None),
        ),
        check_vma=False,
    )
```

profile of v0, /device:TPU:2, one launch (start us, length us, event | category | flops | bytes accessed | tf_op | source)
XLA Modules:
  0.0 270.8 jit_solution(16528090919166589030)
XLA Ops:
  7.2 0.0 copy-start
  7.2 1.3 convolution_convert_fusion.2
  8.5 0.2 copy.22
  8.7 0.0 copy-start.3
  8.7 18.1 %all_to_all.36 = bf16[8,128,128]{2,0,1:T(8,128)(2,1)S(1)} all-to-all(bf16[8,128,128]{2,0,1:T(8,128)(2,1)S(1)} %copy.22), channel_id=1, replica_groups=mesh['dp'=32,'mp'=16] {'mp'}, dimensions={1} | all-to-all | bytes 524288 | tf_op jit(solution)/shard_map/all_to_all | solution.py:30
  26.9 0.0 copy-done
  26.9 0.0 copy-done.3
  26.9 1.3 fusion.4
  28.2 0.3 fusion.1
  28.5 0.9 copy.26
  29.4 5.1 %all-to-all-start.1 = ((bf16[128,8,128]{2,1,0:T(8,128)(2,1)}), bf16[128,8,128]{2,1,0:T(8,128)(2,1)S(1)}, u32[]{:S(2)}, u32[]{:S(2)}) async-start(bf16[128,8,128]{2,1,0:T(8,128)(2,1)} %copy.26), calls=%async_computation.1 | async-start | bytes 524288 | tf_op jit(solution)/shard_map/all_to_all | solution.py:70
  34.6 0.0 reduce-scatter.5.cloned.1.call-start
  34.6 0.3 convolution_multiply_fusion
  34.9 1.1 copy.29
  36.0 0.0 copy-start.2
  36.0 0.0 reduce-scatter.5.cloned.1.call-update
  36.0 0.0 reduce-scatter.3.cloned.1.call-start
  36.1 7.1 %all-to-all-done.1 = bf16[128,8,128]{2,1,0:T(8,128)(2,1)S(1)} async-done(((bf16[128,8,128]{2,1,0:T(8,128)(2,1)}), bf16[128,8,128]{2,1,0:T(8,128)(2,1)S(1)}, u32[]{:S(2)}, u32[]{:S(2)}) %all-to-all-start.1) | async-done | bytes 262176 | tf_op jit(solution)/shard_map/all_to_all | solution.py:70
  43.2 0.0 copy-done.2
  43.2 0.3 fusion
  43.5 1.0 copy.28
  44.5 0.0 copy-start.1
  44.5 0.0 reduce-scatter.3.cloned.1.call-update
  44.5 108.3 %reduce-scatter.5.cloned.1.call-done = f32[8,4,128]{2,0,1:T(8,128)} async-done(((f32[8,128,128]{2,0,1:T(8,128)}), f32[8,4,128]{2,0,1:T(8,128)}) %reduce-scatter.5.cloned.1.call-update) | async-done | bytes 16400 | tf_op jit(solution)/shard_map/reduce_scatter | solution.py:60
  152.8 1.3 copy.31
  154.1 0.0 copy-done.1
  154.1 0.9 convolution_convert_fusion
  155.0 107.7 %reduce-scatter.3.cloned.1.call-done = f32[8,4,128]{2,0,1:T(8,128)} async-done(((f32[8,128,128]{2,0,1:T(8,128)}), f32[8,4,128]{2,0,1:T(8,128)}) %reduce-scatter.3.cloned.1.call-update) | async-done | bytes 16400 | tf_op jit(solution)/shard_map/reduce_scatter | solution.py:76
  262.7 1.3 copy.30
Async XLA Ops:
  7.2 19.7 %copy-start = (bf16[1,8,128,128]{3,2,1,0:T(8,128)(2,1)S(1)}, bf16[1,8,128,128]{3,2,1,0:T(8,128)(2,1)}, u32[]{:S(2)}) copy-start(bf16[1,8,128,128]{3,2,1,0:T(8,128)(2,1)} %param.7) | copy-start | bytes 786436
  8.7 18.2 %copy-start.3 = (bf16[1024,128]{1,0:T(8,128)(2,1)S(1)}, bf16[1024,128]{1,0:T(8,128)(2,1)}, u32[]{:S(2)}) copy-start(bf16[1024,128]{1,0:T(8,128)(2,1)} %param.5) | copy-start | bytes 786436
  29.4 13.8 %all-to-all-start.1 = ((bf16[128,8,128]{2,1,0:T(8,128)(2,1)}), bf16[128,8,128]{2,1,0:T(8,128)(2,1)S(1)}, u32[]{:S(2)}, u32[]{:S(2)}) async-start(bf16[128,8,128]{2,1,0:T(8,128)(2,1)} %copy.26), calls=%async_computation.1 | async-start | bytes 524288 | tf_op jit(solution)/shard_map/all_to_all | solution.py:70
  34.6 118.2 %reduce-scatter.5.cloned.1.call-start = ((), (), s32[]{:S(2)}) async-start(), calls=%async_computation.5 | async-start | bytes 540672 | tf_op jit(solution)/shard_map/reduce_scatter | solution.py:60
  36.0 7.2 %copy-start.2 = (bf16[1024,128]{1,0:T(8,128)(2,1)S(1)}, bf16[1024,128]{1,0:T(8,128)(2,1)}, u32[]{:S(2)}) copy-start(bf16[1024,128]{1,0:T(8,128)(2,1)} %param.4) | copy-start | bytes 786436
  36.0 226.7 %reduce-scatter.3.cloned.1.call-start = ((), (), s32[]{:S(2)}) async-start(), calls=%async_computation.4 | async-start | bytes 540672 | tf_op jit(solution)/shard_map/reduce_scatter | solution.py:76
  44.5 109.6 %copy-start.1 = (bf16[1,8,128,128]{3,2,1,0:T(8,128)(2,1)S(1)}, bf16[1,8,128,128]{3,2,1,0:T(8,128)(2,1)}, u32[]{:S(2)}) copy-start(bf16[1,8,128,128]{3,2,1,0:T(8,128)(2,1)} %param.6) | copy-start | bytes 786436
Sparse Core Ops, SparseCore 0:
  39.7 113.0 reduce-scatter.4
  157.1 105.5 reduce-scatter.2
where the time goes:
time: 271 us
  waiting for transfers between devices  223 us (82%)
  blocking collectives  18.1 us (7%)
  between operations  14.1 us (5%)
  local copies, waits for them, and re-layouts  5.83 us (2%)
  starting transfers between devices  5.21 us (2%)
  matrix products  4.5 us (2%)
    reduce_scatter x1, waiting for transfers between devices, shards(): lax.psum_scatter(term_l, 'dp', scatter_dimension=1, tiled=True)  108 us
    reduce_scatter x1, waiting for transfers between devices, shards(): lax.psum_scatter(term_r, 'dp', scatter_dimension=1, tiled=True)  108 us
    all_to_all x1, blocking collectives, forward_layer(): lax.all_to_all(first_out, 'mp', split_axis=1, concat_axis=0, tiled=True)  18.1 us
    all_to_all x1, waiting for transfers between devices, shards(): lax.all_to_all(grad_first, 'mp', split_axis=0, concat_axis=1, tiled=True)  7.1 us
  transfers between devices with their start and end apart: 3, of which 3 were waited for; matrix products, arithmetic and copies ran while one was open for 2% of the time, Pallas kernels for 0%

commit v1 on v0

--- a/solution.py
+++ b/solution.py
@@ -27,7 +27,13 @@
 def forward_layer(current, right, left):
     first_out = first_product(current, right)
     return left_apply(
-        left, lax.all_to_all(first_out, "mp", split_axis=1, concat_axis=0, tiled=True)
+        left,
+        jnp.concatenate(
+            lax.all_to_all(
+                jnp.stack(jnp.split(first_out, lax.axis_size("mp"), axis=1)), "mp", 0, 0
+            ),
+            axis=0,
+        ),
     )
 
 

time: 271 us -> 271 us (level)
  no operation moved by 1% of the time
where the time goes in v1:
time: 271 us
  waiting for transfers between devices  223 us (82%)
  blocking collectives  18.1 us (7%)
  between operations  14.2 us (5%)
  local copies, waits for them, and re-layouts  5.86 us (2%)
  starting transfers between devices  5.23 us (2%)
  matrix products  4.49 us (2%)
    reduce_scatter x1, waiting for transfers between devices, shards(): lax.psum_scatter(term_l, 'dp', scatter_dimension=1, tiled=True)  108 us
    reduce_scatter x1, waiting for transfers between devices, shards(): lax.psum_scatter(term_r, 'dp', scatter_dimension=1, tiled=True)  108 us
    all_to_all x1, blocking collectives, forward_layer(): lax.all_to_all(jnp.stack(jnp.split(first_out, lax.axis_size('mp'), axis=1...  18.1 us
    all_to_all x1, waiting for transfers between devices, shards(): lax.all_to_all(grad_first, 'mp', split_axis=0, concat_axis=1, tiled=True)  7.1 us
  transfers between devices with their start and end apart: 3, of which 3 were waited for; matrix products, arithmetic and copies ran while one was open for 2% of the time, Pallas kernels for 0%

profile of v1, /device:TPU:2, one launch (start us, length us, event | category | flops | bytes accessed | tf_op | source)
XLA Modules:
  0.0 271.0 jit_solution(5714630141937464084)
XLA Ops:
  7.2 0.0 copy-start
  7.2 1.3 convolution_convert_fusion.2
  8.8 0.0 copy-start.3
  8.9 18.1 %all_to_all.23 = bf16[16,8,8,128]{3,2,1,0:T(8,128)(2,1)S(1)} all-to-all(bf16[16,8,8,128]{3,2,1,0:T(8,128)(2,1)S(1)} %constant_dynamic-update-slice_fusion), channel_id=1, replica_groups=mesh['dp'=32,'mp'=16] {'mp'}, dimensions={0} | all-to-all | bytes 524288 | tf_op jit(solution)/shard_map/all_to_all | solution.py:32
  27.0 0.0 copy-done
  27.0 0.0 copy-done.3
  27.0 1.3 fusion.4
  28.3 0.3 fusion.1
  28.6 0.9 copy.27
  29.5 5.1 %all-to-all-start.1 = ((bf16[128,8,128]{2,1,0:T(8,128)(2,1)}), bf16[128,8,128]{2,1,0:T(8,128)(2,1)S(1)}, u32[]{:S(2)}, u32[]{:S(2)}) async-start(bf16[128,8,128]{2,1,0:T(8,128)(2,1)} %copy.27), calls=%async_computation.1 | async-start | bytes 524288 | tf_op jit(solution)/shard_map/all_to_all | solution.py:76
  34.7 0.0 reduce-scatter.5.cloned.1.call-start
  34.7 0.3 convolution_multiply_fusion
  35.0 1.1 copy.31
  36.1 0.0 copy-start.2
  36.1 0.0 reduce-scatter.5.cloned.1.call-update
  36.2 0.0 reduce-scatter.3.cloned.1.call-start
  36.2 7.1 %all-to-all-done.1 = bf16[128,8,128]{2,1,0:T(8,128)(2,1)S(1)} async-done(((bf16[128,8,128]{2,1,0:T(8,128)(2,1)}), bf16[128,8,128]{2,1,0:T(8,128)(2,1)S(1)}, u32[]{:S(2)}, u32[]{:S(2)}) %all-to-all-start.1) | async-done | bytes 262176 | tf_op jit(solution)/shard_map/all_to_all | solution.py:76
  43.3 0.0 copy-done.2
  43.3 0.3 fusion
  43.6 1.0 copy.29
  44.6 0.0 copy-start.1
  44.6 0.0 reduce-scatter.3.cloned.1.call-update
  44.6 108.3 %reduce-scatter.5.cloned.1.call-done = f32[8,4,128]{2,0,1:T(8,128)} async-done(((f32[8,128,128]{2,0,1:T(8,128)}), f32[8,4,128]{2,0,1:T(8,128)}) %reduce-scatter.5.cloned.1.call-update) | async-done | bytes 16400 | tf_op jit(solution)/shard_map/reduce_scatter | solution.py:66
  152.9 1.3 copy.33
  154.3 0.0 copy-done.1
  154.3 0.9 convolution_convert_fusion
  155.2 107.6 %reduce-scatter.3.cloned.1.call-done = f32[8,4,128]{2,0,1:T(8,128)} async-done(((f32[8,128,128]{2,0,1:T(8,128)}), f32[8,4,128]{2,0,1:T(8,128)}) %reduce-scatter.3.cloned.1.call-update) | async-done | bytes 16400 | tf_op jit(solution)/shard_map/reduce_scatter | solution.py:82
  262.8 1.3 copy.32
  (16 shorter events, 0.2 us)
Async XLA Ops:
  7.2 19.8 %copy-start = (bf16[1,8,128,128]{3,2,1,0:T(8,128)(2,1)S(1)}, bf16[1,8,128,128]{3,2,1,0:T(8,128)(2,1)}, u32[]{:S(2)}) copy-start(bf16[1,8,128,128]{3,2,1,0:T(8,128)(2,1)} %param.7) | copy-start | bytes 786436
  8.8 18.2 %copy-start.3 = (bf16[1024,128]{1,0:T(8,128)(2,1)S(1)}, bf16[1024,128]{1,0:T(8,128)(2,1)}, u32[]{:S(2)}) copy-start(bf16[1024,128]{1,0:T(8,128)(2,1)} %param.5) | copy-start | bytes 786436
  29.5 13.8 %all-to-all-start.1 = ((bf16[128,8,128]{2,1,0:T(8,128)(2,1)}), bf16[128,8,128]{2,1,0:T(8,128)(2,1)S(1)}, u32[]{:S(2)}, u32[]{:S(2)}) async-start(bf16[128,8,128]{2,1,0:T(8,128)(2,1)} %copy.27), calls=%async_computation.1 | async-start | bytes 524288 | tf_op jit(solution)/shard_map/all_to_all | solution.py:76
  34.7 118.3 %reduce-scatter.5.cloned.1.call-start = ((), (), s32[]{:S(2)}) async-start(), calls=%async_computation.5 | async-start | bytes 540672 | tf_op jit(solution)/shard_map/reduce_scatter | solution.py:66
  36.1 7.2 %copy-start.2 = (bf16[1024,128]{1,0:T(8,128)(2,1)S(1)}, bf16[1024,128]{1,0:T(8,128)(2,1)}, u32[]{:S(2)}) copy-start(bf16[1024,128]{1,0:T(8,128)(2,1)} %param.4) | copy-start | bytes 786436
  36.2 226.6 %reduce-scatter.3.cloned.1.call-start = ((), (), s32[]{:S(2)}) async-start(), calls=%async_computation.4 | async-start | bytes 540672 | tf_op jit(solution)/shard_map/reduce_scatter | solution.py:82
  44.6 109.7 %copy-start.1 = (bf16[1,8,128,128]{3,2,1,0:T(8,128)(2,1)S(1)}, bf16[1,8,128,128]{3,2,1,0:T(8,128)(2,1)}, u32[]{:S(2)}) copy-start(bf16[1,8,128,128]{3,2,1,0:T(8,128)(2,1)} %param.6) | copy-start | bytes 786436
Sparse Core Ops, SparseCore 0:
  39.8 113.0 reduce-scatter.4
  157.3 105.4 reduce-scatter.2
